TPU v7x, 32 devices: a whole 2x2x4 slice. The times are simulated.
32 devices in a mesh: row: 8 (over y, x, core), col: 4 (over z).
Axes of the slice: x: 2, y: 2, z: 4, core: 2. Of those that a mesh axis runs over, the one named last changes fastest.
Arguments:
- pair: bfloat16 [256, 256, 128], P('row', 'col'), may hold values from -6 to 6
- mask: int32 [256], replicated, may hold values 0 or 1
- w_agate: bfloat16 [128, 128], replicated, may hold values from -0.5 to 0.5
- w_aproj: bfloat16 [128, 128], replicated, may hold values from -0.5 to 0.5
- w_bgate: bfloat16 [128, 128], replicated, may hold values from -0.5 to 0.5
- w_bproj: bfloat16 [128, 128], replicated, may hold values from -0.5 to 0.5
- w_gate: bfloat16 [128, 128], replicated, may hold values from -0.5 to 0.5
- w_out: bfloat16 [128, 128], replicated, may hold values from -0.5 to 0.5
- w_up: bfloat16 [128, 512], replicated, may hold values from -0.5 to 0.5
- w_down: bfloat16 [512, 128], replicated, may hold values from -0.25 to 0.25
Outputs:
- updated: bfloat16 [256, 256, 128], P('row', 'col')
All inputs are finite; a program needn't handle non-finite values.
Results may differ from a plain program's by a relative error of at most 0.0059.
Values may be sent and summed in bfloat16 or wider, within the bound.
No kernel may reach another device: no remote copies, remote signals or barrier semaphores. Data moves between devices by JAX's collectives and lax.ppermute only.
A program may use at most 64 MiB of HBM per device.

v0:
```python
import jax
import jax.numpy as jnp
from jax import lax
from jax.sharding import PartitionSpec as P


def layer_norm(values):
    center = values - jnp.mean(values, axis=-1, keepdims=True)
    spread = jnp.mean(center * center, axis=-1, keepdims=True)
    return center * lax.rsqrt(spread + 1e-05)


def body(pair, mask, w_agate, w_aproj, w_bgate, w_bproj, w_gate, w_out, w_up, w_down):
    rows, cols, width = pair.shape
    present = mask.astype(jnp.float32)
    row_start = lax.axis_index("row") * rows
    col_start = lax.axis_index("col") * cols
    row_mask = lax.dynamic_slice_in_dim(present, row_start, rows, 0)
    col_mask = lax.dynamic_slice_in_dim(present, col_start, cols, 0)
    pair_mask = (row_mask[:, None] * col_mask[None, :]).reshape(rows * cols, 1)
    pair_flat = pair.astype(jnp.float32).reshape(rows * cols, width)
    normed = layer_norm(pair_flat).astype(jnp.bfloat16)
    gate = jax.nn.sigmoid(jnp.dot(normed, w_gate, preferred_element_type=jnp.float32))
    left = (
        jax.nn.sigmoid(jnp.dot(normed, w_agate, preferred_element_type=jnp.float32))
        * jnp.dot(normed, w_aproj, preferred_element_type=jnp.float32)
        * pair_mask
    )
    right = (
        jax.nn.sigmoid(jnp.dot(normed, w_bgate, preferred_element_type=jnp.float32))
        * jnp.dot(normed, w_bproj, preferred_element_type=jnp.float32)
        * pair_mask
    )
    left_major = jnp.transpose(left.astype(jnp.bfloat16).reshape(rows, cols, -1), (2, 0, 1))
    right_major = jnp.transpose(right.astype(jnp.bfloat16).reshape(rows, cols, -1), (2, 0, 1))
    left_spread, right_spread = (
        lax.all_to_all(
            lax.all_to_all(left_major, "row", split_axis=0, concat_axis=1, tiled=True),
            "col",
            split_axis=1,
            concat_axis=2,
            tiled=True,
        ),
        lax.all_to_all(
            lax.all_to_all(right_major, "row", split_axis=0, concat_axis=1, tiled=True),
            "col",
            split_axis=1,
            concat_axis=2,
            tiled=True,
        ),
    )
    mixed = jnp.einsum(
        "cik,cjk->cij",
        lax.all_gather(left_spread, "col", axis=1, tiled=True),
        right_spread,
        preferred_element_type=jnp.float32,
    ).astype(jnp.bfloat16)
    mixed = lax.all_to_all(mixed, "row", split_axis=1, concat_axis=0, tiled=True)
    mixed_rows = jnp.transpose(mixed, (1, 2, 0)).astype(jnp.float32).reshape(rows * cols, -1)
    mixed_normed = layer_norm(mixed_rows).astype(jnp.bfloat16)
    middle = pair_flat + gate * jnp.dot(mixed_normed, w_out, preferred_element_type=jnp.float32)
    trans_in = layer_norm(middle).astype(jnp.bfloat16)
    trans_hidden = jax.nn.relu(jnp.dot(trans_in, w_up, preferred_element_type=jnp.float32)).astype(
        jnp.bfloat16
    )
    result = middle + jnp.dot(trans_hidden, w_down, preferred_element_type=jnp.float32)
    return result.astype(jnp.bfloat16).reshape(rows, cols, width)


def solution(mesh):
    placed = (P("row", "col", None), P(), P(), P(), P(), P(), P(), P(), P(), P())
    return jax.shard_map(
        body, mesh=mesh, in_specs=placed, out_specs=P("row", "col", None), check_vma=False
    )
```

profile of v0, /device:TPU:0, one launch (start us, length us, event | category | flops | bytes accessed | tf_op | source)
XLA Modules:
  0.0 144.5 jit_solution(13755586689063979857)
XLA Ops:
  6.5 1.4 convert_reduce_fusion
  8.0 1.7 %multiply_reduce_fusion.2 = f32[32,64]{1,0:T(8,128)S(1)} fusion(bf16[32,64,128]{2,1,0:T(8,128)(2,1)} %param.10, f32[32,64]{1,0:T(8,128)S(1)} %broadcast_multiply_fusion.2), kind=kLoop, calls=%fused_computation.36 | loop fusion | flops 1046528 | bytes 540672 | tf_op jit(solution)/shard_map/reduce_sum | solution.py:9
  10.8 1.6 %fusion.18 = bf16[2048,128]{1,0:T(8,128)(2,1)S(1)} fusion(bf16[32,64,128]{2,1,0:T(8,128)(2,1)} %param.10, f32[2048]{0:T(1024)S(1)} %rsqrt.31, f32[2048]{0:T(1024)S(1)} %div.32), kind=kLoop, calls=%fused_computation.33 | loop fusion | flops 1048576 | bytes 1064960 | tf_op jit(solution)/shard_map/convert_element_type | solution.py:22
  13.6 1.6 %copy.22 = bf16[32,64,128]{1,0,2:T(8,128)(2,1)S(1)} copy(bf16[32,64,128]{2,1,0:T(8,128)(2,1)S(1)} %bitcast.89) | data formatting | bytes 1048576 | tf_op jit(solution)/shard_map/reshape | solution.py:34
  15.9 14.7 %all_to_all.81 = bf16[8,2,16384]{2,1,0:T(2,128)(2,1)S(1)} all-to-all(bf16[8,2,16384]{2,1,0:T(2,128)(2,1)S(1)} %reshape.119), channel_id=1, replica_groups=mesh['row'=8,'col'=4] {'row'}, dimensions={0} | all-to-all | bytes 1048576 | tf_op jit(solution)/shard_map/all_to_all | solution.py:38
  32.1 0.9 reshape.121
  33.0 18.5 %all_to_all.82 = bf16[4,2,32768]{2,1,0:T(2,128)(2,1)S(1)} all-to-all(bf16[4,2,32768]{2,1,0:T(2,128)(2,1)S(1)} %reshape.121), channel_id=1, replica_groups=mesh['row'=8,'col'=4] {'col'}, dimensions={0} | all-to-all | bytes 1048576 | tf_op jit(solution)/shard_map/all_to_all | solution.py:37
  52.2 0.8 copy.45
  53.0 1.5 %all_to_all.66 = bf16[16,64,256]{2,1,0:T(8,128)(2,1)} reshape(bf16[16,64,4,64]{3,2,1,0:T(4,128)(2,1)S(1)} %bitcast.81) | data formatting | bytes 1048576 | tf_op jit(solution)/shard_map/all_to_all | solution.py:37
  55.7 1.6 %copy.27 = bf16[32,64,128]{1,0,2:T(8,128)(2,1)S(1)} copy(bf16[32,64,128]{2,1,0:T(8,128)(2,1)S(1)} %bitcast.88) | data formatting | bytes 1048576 | tf_op jit(solution)/shard_map/reshape | solution.py:35
  58.0 12.2 %all_to_all.83 = bf16[8,2,16384]{2,1,0:T(2,128)(2,1)S(1)} all-to-all(bf16[8,2,16384]{2,1,0:T(2,128)(2,1)S(1)} %reshape.123), channel_id=1, replica_groups=mesh['row'=8,'col'=4] {'row'}, dimensions={0} | all-to-all | bytes 1048576 | tf_op jit(solution)/shard_map/all_to_all | solution.py:45
  71.6 0.9 reshape.125
  72.5 31.4 %all_to_all.84 = bf16[4,2,32768]{2,1,0:T(2,128)(2,1)S(1)} all-to-all(bf16[4,2,32768]{2,1,0:T(2,128)(2,1)S(1)} %reshape.125), channel_id=1, replica_groups=mesh['row'=8,'col'=4] {'col'}, dimensions={0} | all-to-all | bytes 1048576 | tf_op jit(solution)/shard_map/all_to_all | solution.py:44
  104.6 0.8 copy.44
  106.1 3.6 %all-gather.2.cloned.1.call-done = bf16[16,256,256]{2,1,0:T(8,128)(2,1)} async-done(((bf16[16,64,256]{2,1,0:T(8,128)(2,1)}), bf16[16,256,256]{2,1,0:T(8,128)(2,1)}) %all-gather.2.cloned.1.call-update) | async-done | bytes 2097168 | tf_op jit(solution)/shard_map/all_gather | solution.py:54
  109.7 2.3 %convolution_convert_fusion = bf16[16,256,64]{1,2,0:T(8,128)(2,1)S(1)} fusion(bf16[16,256,256]{2,1,0:T(8,128)(2,1)} %all-gather.2.cloned.1.call-done, bf16[16,64,256]{2,1,0:T(8,128)(2,1)S(1)} %all_to_all.74), kind=kOutput, calls=%fused_computation.25 | convolution fusion | flops 134479872 | bytes 3145728 | tf_op jit(solution)/shard_map/cik,cjk->cij/dot_general | solution.py:52
  112.0 1.0 copy.32
  113.0 1.5 %reshape.127 = bf16[8,2,16384]{2,1,0:T(2,128)(2,1)} reshape(bf16[256,16,64]{2,1,0:T(8,128)(2,1)S(1)} %bitcast.76) | data formatting | bytes 1048576
  114.5 3.7 %all-to-all-start.4 = ((bf16[8,2,16384]{2,1,0:T(2,128)(2,1)}), bf16[8,2,16384]{2,1,0:T(2,128)(2,1)S(1)}, u32[]{:S(2)}, u32[]{:S(2)}) async-start(bf16[8,2,16384]{2,1,0:T(2,128)(2,1)} %reshape.127), calls=%async_computation.4 | async-start | bytes 1048576 | tf_op jit(solution)/shard_map/all_to_all | solution.py:58
  118.2 1.4 fusion.11
  119.6 8.3 %all-to-all-done.4 = bf16[8,2,16384]{2,1,0:T(2,128)(2,1)S(1)} async-done(((bf16[8,2,16384]{2,1,0:T(2,128)(2,1)}), bf16[8,2,16384]{2,1,0:T(2,128)(2,1)S(1)}, u32[]{:S(2)}, u32[]{:S(2)}) %all-to-all-start.4) | async-done | bytes 524320 | tf_op jit(solution)/shard_map/all_to_all | solution.py:58
  130.1 2.3 %copy.35 = f32[32,64,128]{2,1,0:T(8,128)} copy(f32[32,64,128]{1,0,2:T(8,128)S(1)} %bitcast.71) | data formatting | bytes 2097152 | tf_op jit(solution)/shard_map/convert_element_type | solution.py:59
  132.4 1.9 %fusion.16 = bf16[2048,128]{1,0:T(8,128)(2,1)S(1)} fusion(f32[32,64,128]{2,1,0:T(8,128)} %copy.35, f32[2048]{0:T(1024)S(1)} %rsqrt.33, f32[2048]{0:T(1024)S(1)} %div.38), kind=kLoop, calls=%fused_computation.28 | loop fusion | flops 786432 | bytes 1589248 | tf_op jit(solution)/shard_map/convert_element_type | solution.py:60
  135.5 2.1 %fusion.14 = bf16[2048,128]{1,0:T(8,128)(2,1)} fusion(f32[2048,128]{1,0:T(8,128)S(1)} %get-tuple-element.6, bf16[512,128]{1,0:T(8,128)(2,1)S(1)} %copy-done, bf16[128,512]{1,0:T(8,128)(2,1)S(1)} %copy-done.6, f32[2048]{0:T(1024)S(1)} %add_rsqrt_fusion.2, f32[2048]{0:T(1024)S(1)} %broadcast_multiply_fusion.3), kind=kOutput, calls=%fused_computation.22 | convolution fusion | flops 540278784 | bytes 1851392 | tf_op jit(solution)/shard_map/dot_general | solution.py:66
  (60 shorter events, 13.0 us)
Async XLA Ops:
  6.5 129.0 %copy-start = (bf16[512,128]{1,0:T(8,128)(2,1)S(1)}, bf16[512,128]{1,0:T(8,128)(2,1)}, u32[]{:S(2)}) copy-start(bf16[512,128]{1,0:T(8,128)(2,1)} %param.19) | copy-start | bytes 393220
  6.5 5.9 %copy-start.7 = (bf16[128,128]{1,0:T(8,128)(2,1)S(1)}, bf16[128,128]{1,0:T(8,128)(2,1)}, u32[]{:S(2)}) copy-start(bf16[128,128]{1,0:T(8,128)(2,1)} %param.12) | copy-start | bytes 98308
  6.5 103.1 %all-gather.2.cloned.1.call-start = ((), (), s32[]{:S(2)}) async-start(), calls=%async_computation.5 | async-start | bytes 2621440 | tf_op jit(solution)/shard_map/all_gather | solution.py:54
  12.5 0.8 copy-start.3
  52.2 2.3 %copy-start.8 = (bf16[128,128]{1,0:T(8,128)(2,1)S(1)}, bf16[128,128]{1,0:T(8,128)(2,1)}, u32[]{:S(2)}) copy-start(bf16[128,128]{1,0:T(8,128)(2,1)} %param.14) | copy-start | bytes 98308
  54.5 0.8 copy-start.4
  112.0 6.2 %copy-start.9 = (bf16[128,128]{1,0:T(8,128)(2,1)S(1)}, bf16[128,128]{1,0:T(8,128)(2,1)}, u32[]{:S(2)}) copy-start(bf16[128,128]{1,0:T(8,128)(2,1)} %param.16) | copy-start | bytes 98308
  114.5 13.4 %all-to-all-start.4 = ((bf16[8,2,16384]{2,1,0:T(2,128)(2,1)}), bf16[8,2,16384]{2,1,0:T(2,128)(2,1)S(1)}, u32[]{:S(2)}, u32[]{:S(2)}) async-start(bf16[8,2,16384]{2,1,0:T(2,128)(2,1)} %reshape.127), calls=%async_computation.4 | async-start | bytes 1048576 | tf_op jit(solution)/shard_map/all_to_all | solution.py:58
  130.0 4.3 %copy-start.1 = (bf16[32,64,128]{2,1,0:T(8,128)(2,1)S(1)}, bf16[32,64,128]{2,1,0:T(8,128)(2,1)}, u32[]{:S(2)}) copy-start(bf16[32,64,128]{2,1,0:T(8,128)(2,1)} %param.10) | copy-start | bytes 1572868
  130.1 4.3 %copy-start.5 = (bf16[128,128]{1,0:T(8,128)(2,1)S(1)}, bf16[128,128]{1,0:T(8,128)(2,1)}, u32[]{:S(2)}) copy-start(bf16[128,128]{1,0:T(8,128)(2,1)} %param.17) | copy-start | bytes 98308
  132.4 1.9 %copy-start.2 = (f32[2048,128]{1,0:T(8,128)S(1)}, f32[2048,128]{1,0:T(8,128)}, u32[]{:S(2)}) copy-start(f32[2048,128]{1,0:T(8,128)} %fusion.11) | copy-start | bytes 3145732
  134.3 1.2 copy-start.6
Sparse Core Ops, SparseCore 0:
  54.6 54.9 all-gather.1
where the time goes:
time: 145 us
  blocking collectives  76.8 us (53%)
  local copies, waits for them, and re-layouts  21.5 us (15%)
  between operations  13.7 us (9%)
  waiting for transfers between devices  11.9 us (8%)
  other arithmetic  8.91 us (6%)
  matrix products  7.95 us (5%)
  starting transfers between devices  3.69 us (3%)
    all_to_all x1, blocking collectives, body(): lax.all_to_all(lax.all_to_all(right_major, 'row', split_axis=0, concat_ax...  31.4 us
    all_to_all x1, blocking collectives, body(): lax.all_to_all(lax.all_to_all(left_major, 'row', split_axis=0, concat_axi...  18.5 us
    all_to_all x1, blocking collectives, body(): lax.all_to_all(left_major, 'row', split_axis=0, concat_axis=1, tiled=True)  14.7 us
    all_to_all x1, blocking collectives, body(): lax.all_to_all(right_major, 'row', split_axis=0, concat_axis=1, tiled=True)  12.2 us
    unnamed x30, local copies, waits for them, and re-layouts  8.68 us
    all_to_all x1, waiting for transfers between devices, body(): lax.all_to_all(mixed, 'row', split_axis=1, concat_axis=0, tiled=True)  8.32 us
    all_to_all x1, starting transfers between devices, body(): lax.all_to_all(mixed, 'row', split_axis=1, concat_axis=0, tiled=True)  3.69 us
    all_gather x1, waiting for transfers between devices, body(): lax.all_gather(left_spread, 'col', axis=1, tiled=True)  3.59 us
  transfers between devices with their start and end apart: 2, of which 2 were waited for; matrix products, arithmetic and copies ran while one was open for 6% of the time, Pallas kernels for 0%

commit v1 on v0

--- a/solution.py
+++ b/solution.py
@@ -49,9 +49,38 @@
             tiled=True,
         ),
     )
+
+    def use_the_pools(array_dim, mine):
+        local_out = lax.axis_index("col")
+        far_arr = lax.axis_size("col")
+        current_block, shaped, known = (far_arr, local_out, mine.shape[array_dim])
+        windows = [
+            hop_no * current_block if q == array_dim else hop_no
+            for q, hop_no in enumerate(mine.shape)
+        ]
+        inter = jnp.zeros(windows, mine.dtype)
+        even = x_next = mine
+        met_up = lax.dynamic_update_slice_in_dim(inter, mine, shaped * known, axis=array_dim)
+        for p in range(1, current_block // 2 + 1):
+            outcome_arr = range(current_block)
+            arr_now = map(lambda q: (q, (q + 1) % current_block), outcome_arr)
+            item_now = list(arr_now)
+            even = lax.ppermute(even, "col", item_now)
+            met_up = lax.dynamic_update_slice_in_dim(
+                met_up, even, (shaped - p) % current_block * known, axis=array_dim
+            )
+            if 2 * p < current_block:
+                u_next = range(current_block)
+                latest = map(lambda q: (q, (q - 1) % current_block), u_next)
+                x_next = lax.ppermute(x_next, "col", list(latest))
+                met_up = lax.dynamic_update_slice_in_dim(
+                    met_up, x_next, (shaped + p) % current_block * known, axis=array_dim
+                )
+        return met_up
+
     mixed = jnp.einsum(
         "cik,cjk->cij",
-        lax.all_gather(left_spread, "col", axis=1, tiled=True),
+        use_the_pools(1, mine=left_spread),
         right_spread,
         preferred_element_type=jnp.float32,
     ).astype(jnp.bfloat16)

time: 145 us -> 134 us (0.924)
  blocking collectives: 76.8 us -> 0 us
  waiting for transfers between devices: 11.9 us -> 53.2 us
  starting transfers between devices: 3.69 us -> 35.2 us
  between operations: 13.7 us -> 0.39 us
  local copies, waits for them, and re-layouts: 21.5 us -> 29.1 us
  matrix products: 7.95 us -> 6.33 us
    all_to_all x4 -> x0, blocking collectives: 76.8 us -> none  [the longest x1 31.4 us: body(): lax.all_to_all(lax.all_to_all(right_major, 'row', split_axis=0, concat_ax...]
    ppermute x0 -> x3, waiting for transfers between devices: none -> 23.6 us  [the longest x2 23.6 us: use_the_pools(): even = lax.ppermute(even, 'col', item_now)]
    all_to_all x0 -> x4, waiting for transfers between devices: none -> 21.3 us  [the longest x1 9.13 us: body(): lax.all_to_all(lax.all_to_all(left_major, 'row', split_axis=0, concat_axi...]
    all_to_all x0 -> x4, starting transfers between devices: none -> 17.2 us  [the longest x1 5.17 us: body(): lax.all_to_all(left_major, 'row', split_axis=0, concat_axis=1, tiled=True)]
    ppermute x0 -> x3, starting transfers between devices: none -> 11.9 us  [the longest x2 9.84 us: use_the_pools(): even = lax.ppermute(even, 'col', item_now)]
    dynamic_update_slice x0 -> x4, local copies, waits for them, and re-layouts: none -> 4.33 us  [the longest x2 2.16 us: use_the_pools(): lax.dynamic_update_slice_in_dim(met_up, even, (shaped - p) % current_bloc...]
    all_gather x1 -> x0, waiting for transfers between devices: 3.59 us -> none  [body(): lax.all_gather(left_spread, 'col', axis=1, tiled=True)]
    unnamed x30, local copies, waits for them, and re-layouts: 8.68 us -> 11.7 us
  transfers between devices with their start and end apart: 2 -> 8, of which waited for: 2 -> 6; matrix products, arithmetic and copies ran while one was open for 6% -> 13% of each run, Pallas kernels for 0% -> 0%
where the time goes in v1:
time: 134 us; the launch traced here: 133 us
  waiting for transfers between devices  53.2 us (40%)
  starting transfers between devices  35.2 us (26%)
  local copies, waits for them, and re-layouts  29.1 us (22%)
  other arithmetic  8.91 us (7%)
  matrix products  6.33 us (5%)
    ppermute x2, waiting for transfers between devices, use_the_pools(): even = lax.ppermute(even, 'col', item_now)  23.6 us
    unnamed x30, local copies, waits for them, and re-layouts  11.7 us
    ppermute x2, starting transfers between devices, use_the_pools(): even = lax.ppermute(even, 'col', item_now)  9.84 us
    all_to_all x1, waiting for transfers between devices, body(): lax.all_to_all(lax.all_to_all(left_major, 'row', split_axis=0, concat_axi...  9.13 us
    all_to_all x1, waiting for transfers between devices, body(): lax.all_to_all(mixed, 'row', split_axis=1, concat_axis=0, tiled=True)  8.35 us
    all_to_all x1, waiting for transfers between devices, body(): lax.all_to_all(right_major, 'row', split_axis=0, concat_axis=1, tiled=True)  6.66 us
    all_to_all x1, starting transfers between devices, body(): lax.all_to_all(mixed, 'row', split_axis=1, concat_axis=0, tiled=True)  6.11 us
    all_to_all x1, waiting for transfers between devices, body(): lax.all_to_all(left_major, 'row', split_axis=0, concat_axis=1, tiled=True)  5.48 us
  transfers between devices with their start and end apart: 8, of which 6 were waited for; matrix products, arithmetic and copies ran while one was open for 13% of the time, Pallas kernels for 0%

profile of v1, /device:TPU:0, one launch (start us, length us, event | category | flops | bytes accessed | tf_op | source)
XLA Modules:
  0.0 133.1 jit_solution(7841551384834888184)
XLA Ops:
  1.4 1.7 %multiply_reduce_fusion.2 = f32[32,64]{1,0:T(8,128)S(1)} fusion(bf16[32,64,128]{2,1,0:T(8,128)(2,1)} %param.10, f32[32,64]{1,0:T(8,128)S(1)} %broadcast_multiply_fusion.2), kind=kLoop, calls=%fused_computation.36 | loop fusion | flops 1046528 | bytes 540672 | tf_op jit(solution)/shard_map/reduce_sum | solution.py:9
  4.3 1.6 %fusion.18 = bf16[2048,128]{1,0:T(8,128)(2,1)S(1)} fusion(bf16[32,64,128]{2,1,0:T(8,128)(2,1)} %param.10, f32[2048]{0:T(1024)S(1)} %rsqrt.31, f32[2048]{0:T(1024)S(1)} %div.32), kind=kLoop, calls=%fused_computation.33 | loop fusion | flops 1048576 | bytes 1064960 | tf_op jit(solution)/shard_map/convert_element_type | solution.py:22
  7.1 1.6 %copy.32 = bf16[32,64,128]{1,0,2:T(8,128)(2,1)S(1)} copy(bf16[32,64,128]{2,1,0:T(8,128)(2,1)S(1)} %bitcast.89) | data formatting | bytes 1048576 | tf_op jit(solution)/shard_map/reshape | solution.py:34
  8.7 1.5 %reshape.119 = bf16[8,2,16384]{2,1,0:T(2,128)(2,1)} reshape(bf16[128,32,64]{2,1,0:T(8,128)(2,1)S(1)} %bitcast.74) | data formatting | bytes 1048576
  10.2 5.2 %all-to-all-start = ((bf16[8,2,16384]{2,1,0:T(2,128)(2,1)}), bf16[8,2,16384]{2,1,0:T(2,128)(2,1)S(1)}, u32[]{:S(2)}, u32[]{:S(2)}) async-start(bf16[8,2,16384]{2,1,0:T(2,128)(2,1)} %reshape.119), calls=%async_computation | async-start | bytes 1048576 | tf_op jit(solution)/shard_map/all_to_all | solution.py:38
  16.5 1.6 %copy.37 = bf16[32,64,128]{1,0,2:T(8,128)(2,1)S(1)} copy(bf16[32,64,128]{2,1,0:T(8,128)(2,1)S(1)} %bitcast.88) | data formatting | bytes 1048576 | tf_op jit(solution)/shard_map/reshape | solution.py:35
  19.6 5.5 %all-to-all-done = bf16[8,2,16384]{2,1,0:T(2,128)(2,1)S(1)} async-done(((bf16[8,2,16384]{2,1,0:T(2,128)(2,1)}), bf16[8,2,16384]{2,1,0:T(2,128)(2,1)S(1)}, u32[]{:S(2)}, u32[]{:S(2)}) %all-to-all-start) | async-done | bytes 524320 | tf_op jit(solution)/shard_map/all_to_all | solution.py:38
  25.1 3.5 %all-to-all-start.2 = ((bf16[8,2,16384]{2,1,0:T(2,128)(2,1)}), bf16[8,2,16384]{2,1,0:T(2,128)(2,1)S(1)}, u32[]{:S(2)}, u32[]{:S(2)}) async-start(bf16[8,2,16384]{2,1,0:T(2,128)(2,1)} %reshape.123), calls=%async_computation.2 | async-start | bytes 1048576 | tf_op jit(solution)/shard_map/all_to_all | solution.py:45
  30.1 1.6 %reshape.121 = bf16[4,2,32768]{2,1,0:T(2,128)(2,1)} reshape(bf16[256,16,64]{2,1,0:T(8,128)(2,1)S(1)} %bitcast.79) | data formatting | bytes 1048576
  31.6 6.7 %all-to-all-done.2 = bf16[8,2,16384]{2,1,0:T(2,128)(2,1)S(1)} async-done(((bf16[8,2,16384]{2,1,0:T(2,128)(2,1)}), bf16[8,2,16384]{2,1,0:T(2,128)(2,1)S(1)}, u32[]{:S(2)}, u32[]{:S(2)}) %all-to-all-start.2) | async-done | bytes 524320 | tf_op jit(solution)/shard_map/all_to_all | solution.py:45
  38.3 4.9 %all-to-all-start.1 = ((bf16[4,2,32768]{2,1,0:T(2,128)(2,1)}), bf16[4,2,32768]{2,1,0:T(2,128)(2,1)S(1)}, u32[]{:S(2)}, u32[]{:S(2)}) async-start(bf16[4,2,32768]{2,1,0:T(2,128)(2,1)} %reshape.121), calls=%async_computation.1 | async-start | bytes 1048576 | tf_op jit(solution)/shard_map/all_to_all | solution.py:37
  44.6 1.5 %reshape.125 = bf16[4,2,32768]{2,1,0:T(2,128)(2,1)} reshape(bf16[256,16,64]{2,1,0:T(8,128)(2,1)S(1)} %bitcast.82) | data formatting | bytes 1048576
  46.2 9.1 %all-to-all-done.1 = bf16[4,2,32768]{2,1,0:T(2,128)(2,1)S(1)} async-done(((bf16[4,2,32768]{2,1,0:T(2,128)(2,1)}), bf16[4,2,32768]{2,1,0:T(2,128)(2,1)S(1)}, u32[]{:S(2)}, u32[]{:S(2)}) %all-to-all-start.1) | async-done | bytes 524320 | tf_op jit(solution)/shard_map/all_to_all | solution.py:37
  55.3 3.6 %all-to-all-start.3 = ((bf16[4,2,32768]{2,1,0:T(2,128)(2,1)}), bf16[4,2,32768]{2,1,0:T(2,128)(2,1)S(1)}, u32[]{:S(2)}, u32[]{:S(2)}) async-start(bf16[4,2,32768]{2,1,0:T(2,128)(2,1)} %reshape.125), calls=%async_computation.3 | async-start | bytes 1048576 | tf_op jit(solution)/shard_map/all_to_all | solution.py:44
  62.0 1.8 %collective-permute-start = (bf16[16,64,256]{2,1,0:T(8,128)(2,1)}, bf16[16,64,256]{2,1,0:T(8,128)(2,1)}, u32[]{:S(2)}, u32[]{:S(2)}) collective-permute-start(bf16[16,64,256]{2,1,0:T(8,128)(2,1)} %all_to_all.66), channel_id=1, source_target_pairs={{0,1},{1,2},{2,3},{3,0},{4,5},{5,6},{6,7},{7,4},{8,9},{9,10},{10,1... | collective-permute-start | bytes 1572872 | tf_op jit(solution)/shard_map/ppermute | solution.py:68
  63.8 2.0 %collective-permute-start.1 = (bf16[16,64,256]{2,1,0:T(8,128)(2,1)}, bf16[16,64,256]{2,1,0:T(8,128)(2,1)}, u32[]{:S(2)}, u32[]{:S(2)}) collective-permute-start(bf16[16,64,256]{2,1,0:T(8,128)(2,1)} %all_to_all.66), channel_id=1, source_target_pairs={{0,3},{1,0},{2,1},{3,2},{4,7},{5,4},{6,5},{7,6},{8,11},{9,8},{10,9... | collective-permute-start | bytes 1572872 | tf_op jit(solution)/shard_map/ppermute | solution.py:75
  65.8 18.4 %collective-permute-done = bf16[16,64,256]{2,1,0:T(8,128)(2,1)} collective-permute-done((bf16[16,64,256]{2,1,0:T(8,128)(2,1)}, bf16[16,64,256]{2,1,0:T(8,128)(2,1)}, u32[]{:S(2)}, u32[]{:S(2)}) %collective-permute-start) | collective-permute-done | bytes 524320 | tf_op jit(solution)/shard_map/ppermute | solution.py:68
  84.2 8.1 %collective-permute-start.2 = (bf16[16,64,256]{2,1,0:T(8,128)(2,1)}, bf16[16,64,256]{2,1,0:T(8,128)(2,1)}, u32[]{:S(2)}, u32[]{:S(2)}) collective-permute-start(bf16[16,64,256]{2,1,0:T(8,128)(2,1)} %collective-permute-done), channel_id=1, source_target_pairs={{0,1},{1,2},{2,3},{3,0},{4,5},{5,6},{6,7},{7,4},{8,9},{9,10},{10,1... | collective-permute-start | bytes 1572872 | tf_op jit(solution)/shard_map/ppermute | solution.py:68
  98.0 5.2 %collective-permute-done.2 = bf16[16,64,256]{2,1,0:T(8,128)(2,1)} collective-permute-done((bf16[16,64,256]{2,1,0:T(8,128)(2,1)}, bf16[16,64,256]{2,1,0:T(8,128)(2,1)}, u32[]{:S(2)}, u32[]{:S(2)}) %collective-permute-start.2) | collective-permute-done | bytes 524320 | tf_op jit(solution)/shard_map/ppermute | solution.py:68
  107.5 6.1 %all-to-all-start.4 = ((bf16[8,2,16384]{2,1,0:T(2,128)(2,1)}), bf16[8,2,16384]{2,1,0:T(2,128)(2,1)S(1)}, u32[]{:S(2)}, u32[]{:S(2)}) async-start(bf16[8,2,16384]{2,1,0:T(2,128)(2,1)} %reshape.127), calls=%async_computation.4 | async-start | bytes 1048576 | tf_op jit(solution)/shard_map/all_to_all | solution.py:87
  115.0 8.3 %all-to-all-done.4 = bf16[8,2,16384]{2,1,0:T(2,128)(2,1)S(1)} async-done(((bf16[8,2,16384]{2,1,0:T(2,128)(2,1)}), bf16[8,2,16384]{2,1,0:T(2,128)(2,1)S(1)}, u32[]{:S(2)}, u32[]{:S(2)}) %all-to-all-start.4) | async-done | bytes 524320 | tf_op jit(solution)/shard_map/all_to_all | solution.py:87
  125.5 2.3 %copy.45 = f32[32,64,128]{2,1,0:T(8,128)} copy(f32[32,64,128]{1,0,2:T(8,128)S(1)} %bitcast.71) | data formatting | bytes 2097152 | tf_op jit(solution)/shard_map/convert_element_type | solution.py:88
  127.8 1.9 %fusion.16 = bf16[2048,128]{1,0:T(8,128)(2,1)S(1)} fusion(f32[32,64,128]{2,1,0:T(8,128)} %copy.45, f32[2048]{0:T(1024)S(1)} %rsqrt.33, f32[2048]{0:T(1024)S(1)} %div.38), kind=kLoop, calls=%fused_computation.28 | loop fusion | flops 786432 | bytes 1589248 | tf_op jit(solution)/shard_map/convert_element_type | solution.py:89
  131.0 2.1 %fusion.14 = bf16[2048,128]{1,0:T(8,128)(2,1)} fusion(f32[2048,128]{1,0:T(8,128)S(1)} %get-tuple-element.6, bf16[512,128]{1,0:T(8,128)(2,1)S(1)} %copy-done, bf16[128,512]{1,0:T(8,128)(2,1)S(1)} %copy-done.6, f32[2048]{0:T(1024)S(1)} %add_rsqrt_fusion.2, f32[2048]{0:T(1024)S(1)} %broadcast_multiply_fusion.3), kind=kOutput, calls=%fused_computation.22 | convolution fusion | flops 540278784 | bytes 1851392 | tf_op jit(solution)/shard_map/dot_general | solution.py:95
  (72 shorter events, 26.8 us)
Async XLA Ops:
  0.0 130.9 %copy-start = (bf16[512,128]{1,0:T(8,128)(2,1)S(1)}, bf16[512,128]{1,0:T(8,128)(2,1)}, u32[]{:S(2)}) copy-start(bf16[512,128]{1,0:T(8,128)(2,1)} %param.19) | copy-start | bytes 393220
  0.0 5.9 %copy-start.7 = (bf16[128,128]{1,0:T(8,128)(2,1)S(1)}, bf16[128,128]{1,0:T(8,128)(2,1)}, u32[]{:S(2)}) copy-start(bf16[128,128]{1,0:T(8,128)(2,1)} %param.12) | copy-start | bytes 98308
  5.9 0.8 copy-start.3
  7.1 8.3 %copy-start.8 = (bf16[128,128]{1,0:T(8,128)(2,1)S(1)}, bf16[128,128]{1,0:T(8,128)(2,1)}, u32[]{:S(2)}) copy-start(bf16[128,128]{1,0:T(8,128)(2,1)} %param.14) | copy-start | bytes 98308
  10.2 14.9 %all-to-all-start = ((bf16[8,2,16384]{2,1,0:T(2,128)(2,1)}), bf16[8,2,16384]{2,1,0:T(2,128)(2,1)S(1)}, u32[]{:S(2)}, u32[]{:S(2)}) async-start(bf16[8,2,16384]{2,1,0:T(2,128)(2,1)} %reshape.119), calls=%async_computation | async-start | bytes 1048576 | tf_op jit(solution)/shard_map/all_to_all | solution.py:38
  15.4 0.8 copy-start.4
  25.1 13.2 %all-to-all-start.2 = ((bf16[8,2,16384]{2,1,0:T(2,128)(2,1)}), bf16[8,2,16384]{2,1,0:T(2,128)(2,1)S(1)}, u32[]{:S(2)}, u32[]{:S(2)}) async-start(bf16[8,2,16384]{2,1,0:T(2,128)(2,1)} %reshape.123), calls=%async_computation.2 | async-start | bytes 1048576 | tf_op jit(solution)/shard_map/all_to_all | solution.py:45
  38.3 17.0 %all-to-all-start.1 = ((bf16[4,2,32768]{2,1,0:T(2,128)(2,1)}), bf16[4,2,32768]{2,1,0:T(2,128)(2,1)S(1)}, u32[]{:S(2)}, u32[]{:S(2)}) async-start(bf16[4,2,32768]{2,1,0:T(2,128)(2,1)} %reshape.121), calls=%async_computation.1 | async-start | bytes 1048576 | tf_op jit(solution)/shard_map/all_to_all | solution.py:37
  55.3 37.0 %all-to-all-start.3 = ((bf16[4,2,32768]{2,1,0:T(2,128)(2,1)}), bf16[4,2,32768]{2,1,0:T(2,128)(2,1)S(1)}, u32[]{:S(2)}, u32[]{:S(2)}) async-start(bf16[4,2,32768]{2,1,0:T(2,128)(2,1)} %reshape.125), calls=%async_computation.3 | async-start | bytes 1048576 | tf_op jit(solution)/shard_map/all_to_all | solution.py:44
  62.0 22.2 %collective-permute-start = (bf16[16,64,256]{2,1,0:T(8,128)(2,1)}, bf16[16,64,256]{2,1,0:T(8,128)(2,1)}, u32[]{:S(2)}, u32[]{:S(2)}) collective-permute-start(bf16[16,64,256]{2,1,0:T(8,128)(2,1)} %all_to_all.66), channel_id=1, source_target_pairs={{0,1},{1,2},{2,3},{3,0},{4,5},{5,6},{6,7},{7,4},{8,9},{9,10},{10,1... | collective-permute-start | bytes 1572872 | tf_op jit(solution)/shard_map/ppermute | solution.py:68
  63.8 33.1 %collective-permute-start.1 = (bf16[16,64,256]{2,1,0:T(8,128)(2,1)}, bf16[16,64,256]{2,1,0:T(8,128)(2,1)}, u32[]{:S(2)}, u32[]{:S(2)}) collective-permute-start(bf16[16,64,256]{2,1,0:T(8,128)(2,1)} %all_to_all.66), channel_id=1, source_target_pairs={{0,3},{1,0},{2,1},{3,2},{4,7},{5,4},{6,5},{7,6},{8,11},{9,8},{10,9... | collective-permute-start | bytes 1572872 | tf_op jit(solution)/shard_map/ppermute | solution.py:75
  84.2 18.9 %collective-permute-start.2 = (bf16[16,64,256]{2,1,0:T(8,128)(2,1)}, bf16[16,64,256]{2,1,0:T(8,128)(2,1)}, u32[]{:S(2)}, u32[]{:S(2)}) collective-permute-start(bf16[16,64,256]{2,1,0:T(8,128)(2,1)} %collective-permute-done), channel_id=1, source_target_pairs={{0,1},{1,2},{2,3},{3,0},{4,5},{5,6},{6,7},{7,4},{8,9},{9,10},{10,1... | collective-permute-start | bytes 1572872 | tf_op jit(solution)/shard_map/ppermute | solution.py:68
  105.0 8.6 %copy-start.9 = (bf16[128,128]{1,0:T(8,128)(2,1)S(1)}, bf16[128,128]{1,0:T(8,128)(2,1)}, u32[]{:S(2)}) copy-start(bf16[128,128]{1,0:T(8,128)(2,1)} %param.16) | copy-start | bytes 98308
  107.5 15.9 %all-to-all-start.4 = ((bf16[8,2,16384]{2,1,0:T(2,128)(2,1)}), bf16[8,2,16384]{2,1,0:T(2,128)(2,1)S(1)}, u32[]{:S(2)}, u32[]{:S(2)}) async-start(bf16[8,2,16384]{2,1,0:T(2,128)(2,1)} %reshape.127), calls=%async_computation.4 | async-start | bytes 1048576 | tf_op jit(solution)/shard_map/all_to_all | solution.py:87
  125.5 4.3 %copy-start.1 = (bf16[32,64,128]{2,1,0:T(8,128)(2,1)S(1)}, bf16[32,64,128]{2,1,0:T(8,128)(2,1)}, u32[]{:S(2)}) copy-start(bf16[32,64,128]{2,1,0:T(8,128)(2,1)} %param.10) | copy-start | bytes 1572868
  125.5 4.3 %copy-start.5 = (bf16[128,128]{1,0:T(8,128)(2,1)S(1)}, bf16[128,128]{1,0:T(8,128)(2,1)}, u32[]{:S(2)}) copy-start(bf16[128,128]{1,0:T(8,128)(2,1)} %param.17) | copy-start | bytes 98308
  127.8 1.9 %copy-start.2 = (f32[2048,128]{1,0:T(8,128)S(1)}, f32[2048,128]{1,0:T(8,128)}, u32[]{:S(2)}) copy-start(f32[2048,128]{1,0:T(8,128)} %fusion.11) | copy-start | bytes 3145732
  129.8 1.2 copy-start.6
